TPU v7x, 32 devices: a whole 2x2x4 slice. The times are simulated.
32 devices in a mesh: seq: 4 (over z), ch: 8 (over y, x, core).
Axes of the slice: x: 2, y: 2, z: 4, core: 2. Of those that a mesh axis runs over, the one named last changes fastest.
Arguments:
- inputs: bfloat16 [1024, 8192], P('seq', 'ch'), may hold values from -6 to 6
- w_in: bfloat16 [3, 8192, 8192], P(None, 'seq', 'ch'), may hold values from -0.0625 to 0.0625
- short_filter: float32 [3, 3, 8192], P(None, None, 'ch'), may hold values from -3 to 3
- rates: float32 [16, 8192], P(None, 'ch'), may hold values from 9.765625e-05 to 0.05
- residues: float32 [16, 8192], P(None, 'ch'), may hold values from -3 to 3
- skip: float32 [8192], P('ch'), may hold values from -3 to 3
Outputs:
- gated: bfloat16 [1024, 8192], P('seq', 'ch')
All inputs are finite; a program needn't handle non-finite values.
Results may differ from a plain program's by a relative error of at most 0.0065.
Values may be sent and summed in bfloat16 or wider, within the bound.
No kernel may reach another device: no remote copies, remote signals or barrier semaphores. Data moves between devices by JAX's collectives and lax.ppermute only.
A program may use at most 128 MiB of HBM per device.

v0:
```python
import jax
import jax.numpy as jnp
from jax import lax
from jax.sharding import PartitionSpec as P

TAPS = 3


def passed_along(block, axis, distance):
    devices = range(lax.axis_size(axis))
    route = [(i - distance, i) for i in devices if i - distance in devices]
    return lax.ppermute(block, axis, route)


def carried_in(part, axis, combine, identity):
    place = lax.axis_index(axis)
    gathered = jax.tree.map(lambda a: lax.all_gather(a, axis), part)
    state = jax.tree.map(lambda a, e: jnp.zeros_like(a) + jnp.asarray(e, a.dtype), part, identity)

    def one(hop, state):
        return combine(
            state, jax.tree.map(lambda a: lax.dynamic_index_in_dim(a, hop, 0, False), gathered)
        )

    return lax.fori_loop(0, place, one, state)


def combine(earlier, later):
    return (earlier[0] * later[0], earlier[1] * later[0] + later[1])


def per_device(inputs, w_in, short_filter, rates, residues, skip):
    tok_rows = inputs.shape[0]
    width = w_in.shape[2]
    modes = rates.shape[0]
    features = lax.all_gather(inputs, "ch", axis=1, tiled=True)
    proj = jnp.einsum(
        "td,kdc->ktc",
        features,
        lax.all_gather(w_in, "seq", axis=1, tiled=True),
        preferred_element_type=jnp.float32,
    ).astype(jnp.bfloat16)
    prior = passed_along(proj[:, tok_rows - (TAPS - 1) :, :], "seq", 1)
    padded = jnp.concatenate([prior, proj], axis=1).astype(jnp.float32)
    mixed = jnp.zeros((3, tok_rows, width), jnp.float32)
    for j in range(TAPS):
        mixed = (
            mixed
            + short_filter[:, j, None, :] * padded[:, TAPS - 1 - j : TAPS - 1 - j + tok_rows, :]
        )
    query, key, value = (mixed[0], mixed[1], mixed[2])
    drive = key * value
    position = jnp.arange(tok_rows, dtype=jnp.float32)
    scaled = residues * jnp.sqrt(1.0 - jnp.exp(-2.0 * rates))
    end_powers = jnp.exp(-rates[None, :, :] * (tok_rows - 1.0 - position)[:, None, None])
    end_state = jnp.sum(end_powers * drive[:, None, :], axis=0)
    block_decay = jnp.exp(-rates * tok_rows)
    identity = (jnp.ones_like(block_decay), jnp.zeros_like(end_state))
    entering = carried_in((block_decay, end_state), "seq", combine, identity)[1]
    start_powers = jnp.exp(-rates[None, :, :] * (position + 1.0)[:, None, None])
    cross = jnp.sum(start_powers * (scaled * entering)[None, :, :], axis=1)
    center = (tok_rows - 1.0) / 2.0
    offset = (position - center)[:, None, None]
    rising = jnp.exp(rates[None, :, :] * offset) * drive[:, None, :]
    offsets = jnp.arange(tok_rows, dtype=jnp.int32)
    lower = (offsets[:, None] >= offsets[None, :]).astype(jnp.float32)
    prefix = jnp.dot(
        lower, rising.reshape(tok_rows, modes * width), precision=lax.Precision.HIGHEST
    )
    prefix = prefix.reshape(tok_rows, modes, width)
    falling = jnp.exp(-rates[None, :, :] * offset) * scaled[None, :, :]
    local = jnp.sum(falling * prefix, axis=1)
    return (query * (local + cross + skip[None, :] * drive)).astype(jnp.bfloat16)


def solution(mesh):
    in_specs = (
        P("seq", "ch"),
        P(None, "seq", "ch"),
        P(None, None, "ch"),
        P(None, "ch"),
        P(None, "ch"),
        P("ch"),
    )
    out_specs = P("seq", "ch")
    return jax.shard_map(
        per_device, mesh=mesh, in_specs=in_specs, out_specs=out_specs, check_vma=False
    )
```

profile of v0, /device:TPU:0, one launch (start us, length us, event | category | flops | bytes accessed | tf_op | source)
XLA Modules:
  0.0 979.4 jit_solution(17450163939474768816)
XLA Ops:
  6.5 0.0 all-gather.7.cloned.1.call-start
  6.5 0.7 all-gather.7.cloned.1.call-update
  7.3 0.0 all-gather.5.cloned.1.call-start
  7.3 0.7 all-gather.5.cloned.1.call-update
  8.0 0.9 fusion.17
  9.0 1.5 fusion.16
  10.5 0.0 copy-start
  10.5 38.1 %all-gather.7.cloned.1.call-done = bf16[256,8192]{1,0:T(8,128)(2,1)} async-done(((bf16[256,1024]{1,0:T(8,128)(2,1)}), bf16[256,8192]{1,0:T(8,128)(2,1)}) %all-gather.7.cloned.1.call-update) | async-done | bytes 4194320 | tf_op jit(solution)/shard_map/all_gather | solution.py:36
  48.6 837.6 %all-gather.5.cloned.1.call-done = bf16[3,8192,1024]{2,1,0:T(8,128)(2,1)} async-done(((bf16[3,2048,1024]{2,1,0:T(8,128)(2,1)}), bf16[3,8192,1024]{2,1,0:T(8,128)(2,1)}) %all-gather.5.cloned.1.call-update) | async-done | bytes 50331664 | tf_op jit(solution)/shard_map/all_gather | solution.py:40
  886.2 21.8 %fusion.7 = bf16[3,256,1024]{2,1,0:T(8,128)(2,1)S(1)} fusion(bf16[3,8192,1024]{2,1,0:T(8,128)(2,1)} %all-gather.5.cloned.1.call-done, bf16[256,8192]{1,0:T(8,128)(2,1)} %all-gather.7.cloned.1.call-done), kind=kOutput, calls=%fused_computation.15 | convolution fusion | flops 12885688320 | bytes 56098816 | tf_op jit(solution)/shard_map/td,kdc->ktc/dot_general | solution.py:37
  908.0 1.3 collective-permute-start
  909.3 14.3 %all-gather = f32[64,1024]{1,0:T(8,128)S(1)} all-gather(f32[16,1024]{1,0:T(8,128)S(1)} %get-tuple-element.63), channel_id=2, replica_groups=mesh['seq'=4,'ch'=8] {'seq'}, dimensions={0}, use_global_device_ids=true | all-gather | bytes 327680 | tf_op jit(solution)/shard_map/all_gather | solution.py:17
  923.6 0.0 copy-done
  923.6 0.6 copy.13
  924.3 0.0 collective-permute-done
  924.3 0.5 maximum_convert_fusion
  924.7 0.9 fusion.2
  925.7 1.2 fusion.10
  926.8 2.5 copy.12
  929.4 4.1 multiply_reduce_fusion.1
  933.5 14.6 %all-gather.1 = f32[64,1024]{1,0:T(8,128)} all-gather(f32[16,1024]{1,0:T(8,128)S(1)} %multiply_reduce_fusion.1), channel_id=3, replica_groups=mesh['seq'=4,'ch'=8] {'seq'}, dimensions={0}, use_global_device_ids=true | all-gather | bytes 327680 | tf_op jit(solution)/shard_map/all_gather | solution.py:17
  948.1 0.2 while.12
  948.3 0.0 copy-start.1
  948.3 0.9 fusion.15
  949.2 3.9 bitcast_multiply_fusion.1
  953.1 0.0 copy-start.2
  953.1 0.0 copy-done.1
  953.1 14.0 %multiply_reduce_fusion.2 = f32[256,1024]{1,0:T(8,128)} fusion(f32[16,1024,256]{2,1,0:T(8,128)S(1)} %bitcast.50, f32[16,1024]{1,0:T(8,128)S(1)} %get-tuple-element.61, f32[256]{0:T(256)S(1)} %iota_add_fusion.1, f32[16,1024]{1,0:T(8,128)S(1)} %copy-done.1), kind=kOutput, calls=%fused_computation.5 | convolution fusion | flops 12901482496 | bytes 17957888 | tf_op jit(solution)/shard_map/dot_general | solution.py:67
  967.2 2.8 multiply_reduce_fusion
  970.0 0.0 copy-done.2
  970.0 2.6 fusion.12
  (7 shorter events, 0.1 us)
Async XLA Ops:
  6.5 42.0 %all-gather.7.cloned.1.call-start = ((), (), s32[]{:S(2)}) async-start(), calls=%async_computation.1 | async-start | bytes 4718592 | tf_op jit(solution)/shard_map/all_gather | solution.py:36
  7.3 878.9 %all-gather.5.cloned.1.call-start = ((), (), s32[]{:S(2)}) async-start(), calls=%async_computation | async-start | bytes 62914560 | tf_op jit(solution)/shard_map/all_gather | solution.py:40
  10.5 913.1 %copy-start = (f32[16,1024]{1,0:T(8,128)S(1)}, f32[16,1024]{1,0:T(8,128)}, u32[]{:S(2)}) copy-start(f32[16,1024]{1,0:T(8,128)} %param.11) | copy-start | bytes 196612
  908.0 16.3 %collective-permute-start = (bf16[3,2,1024]{2,1,0:T(2,128)(2,1)S(1)}, bf16[3,2,1024]{2,1,0:T(2,128)(2,1)S(1)}, u32[]{:S(2)}, u32[]{:S(2)}) collective-permute-start(bf16[3,2,1024]{2,1,0:T(2,128)(2,1)S(1)} %slice.40), channel_id=1, source_target_pairs={{0,8},{8,16},{16,24},{1,9},{9,17},{17,25},{2,10},{10,18},{18,26},{... | collective-permute-start | bytes 36872 | tf_op jit(solution)/shard_map/ppermute | solution.py:12
  948.3 4.8 copy-start.1
  953.1 16.9 %copy-start.2 = (f32[1024]{0:T(1024)S(1)}, f32[1024]{0:T(1024)}, u32[]{:S(2)}) copy-start(f32[1024]{0:T(1024)} %param.13) | copy-start | bytes 12292
Sparse Core Ops, SparseCore 0:
  9.2 39.2 all-gather.6
  50.1 835.9 all-gather.4
where the time goes:
time: 980 us; the launch traced here: 979 us
  waiting for transfers between devices  877 us (89%)
  matrix products  35.8 us (4%)
  blocking collectives  28.9 us (3%)
  other arithmetic  18.4 us (2%)
  between operations  13.5 us (1%)
    all_gather x1, waiting for transfers between devices, per_device(): lax.all_gather(w_in, 'seq', axis=1, tiled=True)  838 us
    all_gather x1, waiting for transfers between devices, per_device(): features = lax.all_gather(inputs, 'ch', axis=1, tiled=True)  38.1 us
    all_gather x2, blocking collectives, carried_in(): gathered = jax.tree.map(lambda a: lax.all_gather(a, axis), part)  28.9 us
    dot_general x1, matrix products, per_device(): jnp.einsum('td,kdc->ktc', features, lax.all_gather(w_in, 'seq', axis=1, t...  21.8 us
  transfers between devices with their start and end apart: 3, of which 2 were waited for; matrix products, arithmetic and copies ran while one was open for 0% of the time, Pallas kernels for 0%

commit v1 on v0

--- a/solution.py
+++ b/solution.py
@@ -4,6 +4,18 @@
 from jax.sharding import PartitionSpec as P
 
 TAPS = 3
+
+
+def summed_around(array, axis, dim, contribution):
+    size, index, extent = (lax.axis_size(axis), lax.axis_index(axis), array.shape[dim])
+    upward = [(i, (i + 1) % size) for i in range(size)]
+    carried, subtotal = (array, None)
+    for step in range(size):
+        coming = lax.ppermute(carried, axis, upward) if step < size - 1 else None
+        take_in = contribution(carried, (index - step) % size * extent)
+        subtotal = take_in if subtotal is None else subtotal + take_in
+        carried = coming
+    return subtotal
 
 
 def passed_along(block, axis, distance):
@@ -34,11 +46,16 @@
     width = w_in.shape[2]
     modes = rates.shape[0]
     features = lax.all_gather(inputs, "ch", axis=1, tiled=True)
-    proj = jnp.einsum(
-        "td,kdc->ktc",
-        features,
-        lax.all_gather(w_in, "seq", axis=1, tiled=True),
-        preferred_element_type=jnp.float32,
+    proj = summed_around(
+        w_in,
+        "seq",
+        1,
+        lambda part_2, start: jnp.einsum(
+            "td,kdc->ktc",
+            lax.dynamic_slice_in_dim(features, start, part_2.shape[1], axis=1),
+            part_2,
+            preferred_element_type=jnp.float32,
+        ),
     ).astype(jnp.bfloat16)
     prior = passed_along(proj[:, tok_rows - (TAPS - 1) :, :], "seq", 1)
     padded = jnp.concatenate([prior, proj], axis=1).astype(jnp.float32)

time: 980 us -> 912 us (0.931)
  waiting for transfers between devices: 877 us -> 796 us
    all_gather x1 -> x0, waiting for transfers between devices: 838 us -> none  [per_device(): lax.all_gather(w_in, 'seq', axis=1, tiled=True)]
    ppermute x0 -> x3, waiting for transfers between devices: none -> 761 us  [summed_around(): coming = lax.ppermute(carried, axis, upward) if step < size - 1 else None]
    dot_general x1 -> x4, matrix products: 21.8 us -> 28.1 us  [per_device(): jnp.einsum('td,kdc->ktc', lax.dynamic_slice_in_dim(features, start, part_...]
  transfers between devices with their start and end apart: 3 -> 5, of which waited for: 2 -> 4; matrix products, arithmetic and copies ran while one was open for 0% -> 3% of each run, Pallas kernels for 0% -> 0%
where the time goes in v1:
time: 912 us; the launch traced here: 911 us
  waiting for transfers between devices  796 us (87%)
  matrix products  42 us (5%)
  blocking collectives  28.7 us (3%)
  other arithmetic  17.1 us (2%)
  between operations  13.7 us (2%)
    ppermute x3, waiting for transfers between devices, summed_around(): coming = lax.ppermute(carried, axis, upward) if step < size - 1 else None  761 us
    all_gather x1, waiting for transfers between devices, per_device(): features = lax.all_gather(inputs, 'ch', axis=1, tiled=True)  35.4 us
    all_gather x2, blocking collectives, carried_in(): gathered = jax.tree.map(lambda a: lax.all_gather(a, axis), part)  28.7 us
    dot_general x4, matrix products, per_device(): jnp.einsum('td,kdc->ktc', lax.dynamic_slice_in_dim(features, start, part_...  28.1 us
  transfers between devices with their start and end apart: 5, of which 4 were waited for; matrix products, arithmetic and copies ran while one was open for 3% of the time, Pallas kernels for 0%

profile of v1, /device:TPU:0, one launch (start us, length us, event | category | flops | bytes accessed | tf_op | source)
XLA Modules:
  0.0 911.2 jit_solution(17279165955757633357)
XLA Ops:
  6.5 0.0 all-gather.4.cloned.1.call-start
  6.5 3.1 collective-permute-start
  9.6 272.6 %collective-permute-done = bf16[3,2048,1024]{2,1,0:T(8,128)(2,1)S(1)} collective-permute-done((bf16[3,2048,1024]{2,1,0:T(8,128)(2,1)}, bf16[3,2048,1024]{2,1,0:T(8,128)(2,1)S(1)}, u32[]{:S(2)}, u32[]{:S(2)}) %collective-permute-start) | collective-permute-done | bytes 12582944 | tf_op jit(solution)/shard_map/ppermute | solution.py:14
  282.2 0.0 copy-start
  282.2 4.6 copy-done
  286.8 0.0 collective-permute-start.1
  286.8 273.4 %collective-permute-done.1 = bf16[3,2048,1024]{2,1,0:T(8,128)(2,1)} collective-permute-done((bf16[3,2048,1024]{2,1,0:T(8,128)(2,1)S(1)}, bf16[3,2048,1024]{2,1,0:T(8,128)(2,1)}, u32[]{:S(2)}, u32[]{:S(2)}) %collective-permute-start.1) | collective-permute-done | bytes 12582944 | tf_op jit(solution)/shard_map/ppermute | solution.py:14
  560.2 0.0 collective-permute-start.2
  560.2 0.0 all-gather.4.cloned.1.call-update
  560.3 0.9 fusion.25
  561.3 1.5 fusion.24
  562.8 35.4 %all-gather.4.cloned.1.call-done = bf16[256,8192]{1,0:T(8,128)(2,1)} async-done(((bf16[256,1024]{1,0:T(8,128)(2,1)}), bf16[256,8192]{1,0:T(8,128)(2,1)}) %all-gather.4.cloned.1.call-update) | async-done | bytes 4194320 | tf_op jit(solution)/shard_map/all_gather | solution.py:48
  598.2 0.0 copy-start.1
  598.2 6.9 fusion.11
  605.0 0.0 copy-done.1
  605.1 6.4 fusion.9
  611.5 6.4 fusion.7
  618.0 0.0 copy-start.3
  618.0 215.0 %collective-permute-done.2 = bf16[3,2048,1024]{2,1,0:T(8,128)(2,1)} collective-permute-done((bf16[3,2048,1024]{2,1,0:T(8,128)(2,1)}, bf16[3,2048,1024]{2,1,0:T(8,128)(2,1)}, u32[]{:S(2)}, u32[]{:S(2)}) %collective-permute-start.2) | collective-permute-done | bytes 12582944 | tf_op jit(solution)/shard_map/ppermute | solution.py:14
  832.9 8.3 fusion.2
  841.3 1.3 collective-permute-start.3
  842.6 13.8 %all-gather = f32[64,1024]{1,0:T(8,128)S(1)} all-gather(f32[16,1024]{1,0:T(8,128)S(1)} %get-tuple-element.63), channel_id=2, replica_groups=mesh['seq'=4,'ch'=8] {'seq'}, dimensions={0}, use_global_device_ids=true | all-gather | bytes 327680 | tf_op jit(solution)/shard_map/all_gather | solution.py:29
  856.4 0.0 copy-done.3
  856.4 0.6 copy.13
  857.0 0.0 collective-permute-done.3
  857.0 0.5 maximum_convert_fusion
  857.5 0.9 fusion
  858.4 0.0 copy-start.4
  858.4 1.2 fusion.3
  859.6 2.5 copy.12
  862.1 0.0 copy-done.4
  862.1 4.1 multiply_reduce_fusion.1
  866.3 14.9 %all-gather.1 = f32[64,1024]{1,0:T(8,128)} all-gather(f32[16,1024]{1,0:T(8,128)S(1)} %multiply_reduce_fusion.1), channel_id=3, replica_groups=mesh['seq'=4,'ch'=8] {'seq'}, dimensions={0}, use_global_device_ids=true | all-gather | bytes 327680 | tf_op jit(solution)/shard_map/all_gather | solution.py:29
  881.2 0.2 while.12
  881.4 0.9 fusion.23
  882.2 0.0 copy-start.5
  882.2 3.9 bitcast_multiply_fusion.1
  886.2 0.0 copy-done.5
  886.2 14.0 %multiply_reduce_fusion.2 = f32[256,1024]{1,0:T(8,128)} fusion(f32[16,1024,256]{2,1,0:T(8,128)S(1)} %bitcast.58, f32[16,1024]{1,0:T(8,128)S(1)} %get-tuple-element.61, f32[256]{0:T(256)S(1)} %iota_add_fusion.1, f32[16,1024]{1,0:T(8,128)S(1)} %copy-done.5), kind=kOutput, calls=%fused_computation.5 | convolution fusion | flops 12901482496 | bytes 17957888 | tf_op jit(solution)/shard_map/dot_general | solution.py:84
  900.2 0.0 copy-start.2
  900.2 0.0 copy-start.6
  900.2 2.8 multiply_reduce_fusion
  903.0 0.0 copy-done.2
  903.0 0.0 copy-done.6
  903.0 1.4 fusion.5
  (7 shorter events, 0.1 us)
Async XLA Ops:
  6.5 591.6 %all-gather.4.cloned.1.call-start = ((), (), s32[]{:S(2)}) async-start(), calls=%async_computation | async-start | bytes 4718592 | tf_op jit(solution)/shard_map/all_gather | solution.py:48
  6.5 275.6 %collective-permute-start = (bf16[3,2048,1024]{2,1,0:T(8,128)(2,1)}, bf16[3,2048,1024]{2,1,0:T(8,128)(2,1)S(1)}, u32[]{:S(2)}, u32[]{:S(2)}) collective-permute-start(bf16[3,2048,1024]{2,1,0:T(8,128)(2,1)} %param.9), channel_id=1, source_target_pairs={{0,8},{8,16},{16,24},{24,0},{1,9},{9,17},{17,25},{25,1},{2,10},{10... | collective-permute-start | bytes 37748744 | tf_op jit(solution)/shard_map/ppermute | solution.py:14
  282.2 4.6 copy-start
  286.8 273.4 %collective-permute-start.1 = (bf16[3,2048,1024]{2,1,0:T(8,128)(2,1)S(1)}, bf16[3,2048,1024]{2,1,0:T(8,128)(2,1)}, u32[]{:S(2)}, u32[]{:S(2)}) collective-permute-start(bf16[3,2048,1024]{2,1,0:T(8,128)(2,1)S(1)} %collective-permute-done), channel_id=1, source_target_pairs={{0,8},{8,16},{16,24},{24,0},{1,9},{9,17},{17,25},{25,1},{2,10},{10... | collective-permute-start | bytes 37748744 | tf_op jit(solution)/shard_map/ppermute | solution.py:14
  560.2 272.8 %collective-permute-start.2 = (bf16[3,2048,1024]{2,1,0:T(8,128)(2,1)}, bf16[3,2048,1024]{2,1,0:T(8,128)(2,1)}, u32[]{:S(2)}, u32[]{:S(2)}) collective-permute-start(bf16[3,2048,1024]{2,1,0:T(8,128)(2,1)} %collective-permute-done.1), channel_id=1, source_target_pairs={{0,8},{8,16},{16,24},{24,0},{1,9},{9,17},{17,25},{25,1},{2,10},{10... | collective-permute-start | bytes 37748744 | tf_op jit(solution)/shard_map/ppermute | solution.py:14
  598.2 6.9 copy-start.1
  618.0 238.4 %copy-start.3 = (f32[16,1024]{1,0:T(8,128)S(1)}, f32[16,1024]{1,0:T(8,128)}, u32[]{:S(2)}) copy-start(f32[16,1024]{1,0:T(8,128)} %param.11) | copy-start | bytes 196612
  841.3 15.8 %collective-permute-start.3 = (bf16[3,2,1024]{2,1,0:T(2,128)(2,1)S(1)}, bf16[3,2,1024]{2,1,0:T(2,128)(2,1)S(1)}, u32[]{:S(2)}, u32[]{:S(2)}) collective-permute-start(bf16[3,2,1024]{2,1,0:T(2,128)(2,1)S(1)} %slice.40), channel_id=1, source_target_pairs={{0,8},{8,16},{16,24},{1,9},{9,17},{17,25},{2,10},{10,18},{18,26},{... | collective-permute-start | bytes 36872 | tf_op jit(solution)/shard_map/ppermute | solution.py:24
  858.4 3.7 copy-start.4
  882.2 3.9 copy-start.5
  900.2 2.8 copy-start.2
  900.2 2.8 copy-start.6
Sparse Core Ops, SparseCore 0:
  560.3 37.8 all-gather.3
